TPU v7x, 128 devices: a whole 4x4x4 slice. The times are simulated.
128 devices in a mesh: seq: 64 (over z, x, y_lo, core), chan: 2 (over y_hi).
Axes of the slice: x: 4, y: 4 (y_hi: 2, y_lo: 2; y = y_hi * 2 + y_lo), z: 4, core: 2. Of those that a mesh axis runs over, the one named last changes fastest.
Arguments:
- signal: bfloat16 [2, 32768, 128], P('chan', 'seq'), may hold values from -6 to 6
- cotangent: bfloat16 [2, 32768, 128], P('chan', 'seq'), may hold values from -6 to 6
- band_freq: int32 [16], replicated, may hold values from 1 to 8191
- w_embed: float32 [32, 64], replicated, may hold values from -2 to 2
- b_embed: float32 [64], replicated, may hold values from -3.140625 to 3.140625
- w_out: float32 [64, 128], P(None, 'chan'), may hold values from -0.75 to 0.75
- decay: float32 [128], P('chan'), may hold values from 0.25 to 16, as said below
Outputs:
- conv_out: bfloat16 [2, 32768, 128], P('chan', 'seq')
- d_signal: bfloat16 [2, 32768, 128], P('chan', 'seq')
- grad_embed: float32 [32, 64], replicated
- grad_bias: float32 [64], replicated
- grad_out: float32 [64, 128], P(None, 'chan')
Inputs may be any that keep to these rules, and one draw needn't show every extreme that they name: decay rates are positive.
All inputs are finite; a program needn't handle non-finite values.
Results may differ from a plain program's by a relative error of at most 0.007.
Values may be sent and summed in bfloat16 or wider, within the bound.
No kernel may reach another device: no remote copies, remote signals or barrier semaphores. Data moves between devices by JAX's collectives and lax.ppermute only.
A program may use at most 192 MiB of HBM per device.

v0:
```python
import math
import jax
import jax.numpy as jnp
from jax import lax
from jax.sharding import PartitionSpec as P

exact_mode = lax.Precision.HIGHEST


def mat_dot(lhs_mat, rhs_mat):
    return jnp.dot(lhs_mat, rhs_mat, preferred_element_type=jnp.float32, precision=exact_mode)


def band_phase(band_freq, places, seq_total):
    upper_part = places // 1024
    lower_part = places % 1024
    partial_turn = upper_part[:, None] * band_freq[None, :] % seq_total
    wrapped = (partial_turn * 1024 + lower_part[:, None] * band_freq[None, :]) % seq_total
    return wrapped.astype(jnp.float32) * (2.0 * math.pi / seq_total)


def filter_parts(places, band_freq, w_embed, b_embed, w_out, decay, seq_total):
    phases = band_phase(band_freq, places, seq_total)
    features = jnp.concatenate([jnp.cos(phases), jnp.sin(phases)], axis=1)
    preact = mat_dot(features, w_embed) + b_embed[None, :]
    hidden = jnp.sin(preact)
    fraction = places.astype(jnp.float32) / seq_total
    envelope = (
        jnp.exp(-decay[None, :] * fraction[:, None]) * jnp.sqrt((1.0 + decay) / seq_total)[None, :]
    )
    taps = mat_dot(hidden, w_out) * envelope
    return (features, preact, hidden, taps, envelope)


def angle_table(rows_idx, cols_idx, modulus):
    wrapped = rows_idx[:, None] * cols_idx[None, :] % modulus
    angles = wrapped.astype(jnp.float32) * (2.0 * math.pi / modulus)
    return (jnp.cos(angles), jnp.sin(angles))


def local(signal, cotangent, band_freq, w_embed, b_embed, w_out, decay):
    devices = lax.axis_size("seq")
    rank_seq = lax.axis_index("seq")
    seg_len = signal.shape[1] * 2
    channels = signal.shape[2] // 2
    block_w = seg_len // devices
    width = block_w * channels
    rows_all = 2 * devices
    pair = rows_all // devices
    seq_total = seg_len * devices
    fft_size = 2 * seq_total
    inv_scale = 1.0 / fft_size
    n_arr = 3
    dev_ids = jnp.arange(devices, dtype=jnp.int32)
    row_ids = jnp.arange(rows_all, dtype=jnp.int32)
    blk_ids = jnp.arange(block_w, dtype=jnp.int32)
    lane_blk = jnp.arange(width, dtype=jnp.int32) // channels
    b_lane = rank_seq * block_w + lane_blk
    src = jnp.stack([signal.reshape(devices, width), cotangent.reshape(devices, width)], axis=1)
    cols = lax.all_to_all(src, "seq", split_axis=0, concat_axis=0, tiled=True)
    places = (dev_ids[:, None] * seg_len + rank_seq * block_w + blk_ids[None, :]).reshape(-1)
    features, preact, hidden, taps, envelope = filter_parts(
        places, band_freq, w_embed, b_embed, w_out, decay, seq_total
    )
    stacked = jnp.concatenate(
        [cols.astype(jnp.float32), taps.reshape(devices, 1, width)], axis=1
    ).reshape(devices, n_arr * width)
    col_cos, col_sin = angle_table(row_ids, dev_ids, rows_all)
    y_re = mat_dot(col_cos, stacked).reshape(rows_all, n_arr, width)
    y_im = -mat_dot(col_sin, stacked).reshape(rows_all, n_arr, width)
    tw_cos, tw_sin = angle_table(row_ids, b_lane, fft_size)
    tw_cos = tw_cos[:, None, :]
    tw_sin = tw_sin[:, None, :]
    t_re = y_re * tw_cos + y_im * tw_sin
    t_im = y_im * tw_cos - y_re * tw_sin
    spec = jnp.stack([t_re, t_im], axis=1)
    spec = lax.all_to_all(spec, "seq", split_axis=0, concat_axis=0, tiled=True)
    q_cos, q_sin = angle_table(dev_ids, dev_ids, devices)
    stage_a = mat_dot(jnp.concatenate([q_cos, q_sin], axis=0), spec.reshape(devices, -1))
    stage_a = stage_a.reshape(2, devices, pair, 2, n_arr, width)
    a_re = stage_a[0, :, :, 0] + stage_a[1, :, :, 1]
    a_im = stage_a[0, :, :, 1] - stage_a[1, :, :, 0]
    mid_cos, mid_sin = angle_table(dev_ids, lane_blk, seg_len)
    mid_cos = mid_cos[:, None, None, :]
    mid_sin = mid_sin[:, None, None, :]
    b_re = (a_re * mid_cos + a_im * mid_sin).reshape(devices, pair, n_arr, block_w, channels)
    b_im = (a_im * mid_cos - a_re * mid_sin).reshape(devices, pair, n_arr, block_w, channels)
    m_cos, m_sin = angle_table(blk_ids, blk_ids, block_w)

    def blk_mix(table, vals):
        return jnp.einsum(
            "mb,qkzbc->qkzmc", table, vals, preferred_element_type=jnp.float32, precision=exact_mode
        )

    s_re = blk_mix(m_cos, b_re) + blk_mix(m_sin, b_im)
    s_im = blk_mix(m_cos, b_im) - blk_mix(m_sin, b_re)
    sig_r, cot_r, tap_r = (s_re[:, :, 0], s_re[:, :, 1], s_re[:, :, 2])
    sig_i, cot_i, tap_i = (s_im[:, :, 0], s_im[:, :, 1], s_im[:, :, 2])
    prod_r = jnp.stack(
        [
            sig_r * tap_r - sig_i * tap_i,
            cot_r * tap_r + cot_i * tap_i,
            cot_r * sig_r + cot_i * sig_i,
        ],
        axis=2,
    )
    prod_i = jnp.stack(
        [
            sig_r * tap_i + sig_i * tap_r,
            cot_i * tap_r - cot_r * tap_i,
            cot_i * sig_r - cot_r * sig_i,
        ],
        axis=2,
    )
    u_re = blk_mix(m_cos, prod_r) - blk_mix(m_sin, prod_i)
    u_im = blk_mix(m_cos, prod_i) + blk_mix(m_sin, prod_r)
    u_re = u_re.reshape(devices, pair, n_arr, width)
    u_im = u_im.reshape(devices, pair, n_arr, width)
    v_re = u_re * mid_cos - u_im * mid_sin
    v_im = u_im * mid_cos + u_re * mid_sin
    v_all = jnp.stack([v_re, v_im]).reshape(2 * devices, -1)
    inv_mat = jnp.concatenate(
        [jnp.concatenate([q_cos, -q_sin], axis=1), jnp.concatenate([q_sin, q_cos], axis=1)], axis=0
    )
    w_all = mat_dot(inv_mat, v_all).reshape(2, devices, pair, n_arr, width)
    b_rows = dev_ids[:, None] * block_w + lane_blk[None, :]
    k1_own = rank_seq * pair + jnp.arange(pair, dtype=jnp.int32)
    ex_ang = b_rows[:, None, :] * k1_own[None, :, None] % fft_size
    ex_ang = ex_ang.astype(jnp.float32) * (2.0 * math.pi / fft_size)
    ex_cos = jnp.cos(ex_ang)[:, :, None, :]
    ex_sin = jnp.sin(ex_ang)[:, :, None, :]
    x_re = w_all[0] * ex_cos - w_all[1] * ex_sin
    x_im = w_all[0] * ex_sin + w_all[1] * ex_cos
    back = jnp.stack([x_re, x_im], axis=1)
    back = lax.all_to_all(back, "seq", split_axis=0, concat_axis=0, tiled=True)
    back = back.reshape(devices, 2, pair, n_arr * width)
    back = jnp.transpose(back, (1, 0, 2, 3)).reshape(2 * rows_all, n_arr * width)
    out_mat = jnp.concatenate([col_cos.T, -col_sin.T], axis=1)
    res = (mat_dot(out_mat, back) * inv_scale).reshape(devices, n_arr, width)
    rows_out = lax.all_to_all(
        res[:, 0:2].astype(jnp.bfloat16), "seq", split_axis=0, concat_axis=0, tiled=True
    )
    conv_out = rows_out[:, 0].reshape(1, seg_len // 2, 2 * channels)
    d_signal = rows_out[:, 1].reshape(1, seg_len // 2, 2 * channels)
    d_taps = res[:, 2].reshape(devices * block_w, channels)
    d_raw = d_taps * envelope
    d_preact = mat_dot(d_raw, w_out.T) * jnp.cos(preact)
    out_part = mat_dot(hidden.T, d_raw)
    embed_part = mat_dot(features.T, d_preact)
    bias_part = jnp.sum(d_preact, axis=0)
    out_sum = lax.psum(out_part, "seq")
    embed_all, bias_all = lax.psum((embed_part, bias_part), ("seq", "chan"))
    norm_scale = 1.0 / math.sqrt(seq_total)
    return (conv_out, d_signal, embed_all * norm_scale, bias_all * norm_scale, out_sum * norm_scale)


def solution(mesh):
    return jax.shard_map(
        local,
        mesh=mesh,
        in_specs=(
            P("chan", "seq", None),
            P("chan", "seq", None),
            P(),
            P(),
            P(),
            P(None, "chan"),
            P("chan"),
        ),
        out_specs=(P("chan", "seq", None), P("chan", "seq", None), P(), P(), P(None, "chan")),
        check_vma=False,
    )
```

profile of v0, /device:TPU:0, one launch (start us, length us, event | category | flops | bytes accessed | tf_op | source)
XLA Modules:
  0.0 615.8 jit_solution(7838954913175535610)
XLA Ops:
  4.4 9.9 %all-to-all-start = ((bf16[64,2,1024]{2,1,0:T(2,128)(2,1)}), bf16[64,2,1024]{2,1,0:T(2,128)(2,1)S(1)}, u32[]{:S(2)}, u32[]{:S(2)}) async-start(bf16[64,2,1024]{2,1,0:T(2,128)(2,1)} %pad_maximum_fusion.14), calls=%async_computation | async-start | bytes 524288 | tf_op jit(solution)/shard_map/all_to_all | solution.py:60
  29.3 4.1 copy.76
  33.4 6.9 %all-to-all-start.1 = ((f32[128,2,3,1024]{3,1,2,0:T(2,128)}), f32[128,2,3,1024]{3,1,2,0:T(2,128)S(1)}, u32[]{:S(2)}, u32[]{:S(2)}) async-start(f32[128,2,3,1024]{3,1,2,0:T(2,128)} %copy.76), calls=%async_computation.1 | async-start | bytes 6291456 | tf_op jit(solution)/shard_map/all_to_all | solution.py:77
  47.2 9.5 %fusion.38 = (f32[64,2,1024]{2,1,0:T(2,128)}, f32[64,2,1024]{2,1,0:T(2,128)}) fusion(s32[2]{0:T(128)S(1)} %iota_add_fusion.1, s32[64,1024]{1,0:T(8,128)S(1)} %broadcast_add_fusion), kind=kLoop, calls=%fused_computation.88 | loop fusion | flops 1835008 | bytes 1310728 | tf_op jit(solution)/shard_map/cos | solution.py:130
  56.8 23.2 %all-to-all-done.1 = f32[128,2,3,1024]{3,1,2,0:T(2,128)S(1)} async-done(((f32[128,2,3,1024]{3,1,2,0:T(2,128)}), f32[128,2,3,1024]{3,1,2,0:T(2,128)S(1)}, u32[]{:S(2)}, u32[]{:S(2)}) %all-to-all-start.1) | async-done | bytes 3145760 | tf_op jit(solution)/shard_map/all_to_all | solution.py:77
  83.7 4.3 reshape.397
  91.8 9.4 %fusion = f32[2,64,2,2,3,1024]{5,1,4,3,2,0:T(8,128)S(1)} fusion(f32[2,64,64,1,1,1]{2,1,5,4,3,0:T(8,128)} %bitcast.98, f32[2,2,3,1024,64]{3,2,1,0,4:T(4,128)} %dot_general.72), kind=kOutput, calls=%fused_computation.6 | convolution fusion | flops 1207959552 | bytes 9469952 | tf_op jit(solution)/shard_map/dot_general | solution.py:11
  110.0 5.5 fusion.51
  132.9 4.7 subtract_bitcast_fusion
  137.6 4.9 reshape.411
  142.5 6.4 %add_bitcast_fusion = f32[64,2,3,16,64]{4,3,2,1,0:T(8,128)} fusion(f32[64,2,3,64,16]{3,4,2,1,0:T(8,128)S(1)} %fusion.3, f32[64,2,1,16,64]{4,3,2,1,0:T(8,128)} %copy-done.5, f32[64,2,1,16,64]{4,3,2,1,0:T(8,128)} %copy-done.6, f32[64,2,1,16,64]{4,3,2,1,0:T(8,128)} %copy-done.4), kind=kOutput, calls=%fused_computation.9 | convolution fusion | flops 76680704 | bytes 4718592 | tf_op jit(solution)/shard_map/mb,qkzbc->qkzmc/dot_general | solution.py:91
  148.9 4.6 reshape.412
  157.1 4.1 copy.85
  161.2 5.0 reshape.400
  174.9 3.9 squeeze.5
  182.9 4.7 copy.86
  187.5 6.6 %all-to-all-start.2 = ((f32[64,2,2,3,1024]{4,2,3,1,0:T(2,128)}), f32[64,2,2,3,1024]{4,2,3,1,0:T(2,128)S(1)}, u32[]{:S(2)}, u32[]{:S(2)}) async-start(f32[64,2,2,3,1024]{4,2,3,1,0:T(2,128)} %copy.86), calls=%async_computation.2 | async-start | bytes 6291456 | tf_op jit(solution)/shard_map/all_to_all | solution.py:135
  194.9 38.9 %all-to-all-done.2 = f32[64,2,2,3,1024]{4,2,3,1,0:T(2,128)S(1)} async-done(((f32[64,2,2,3,1024]{4,2,3,1,0:T(2,128)}), f32[64,2,2,3,1024]{4,2,3,1,0:T(2,128)S(1)}, u32[]{:S(2)}, u32[]{:S(2)}) %all-to-all-start.2) | async-done | bytes 3145760 | tf_op jit(solution)/shard_map/all_to_all | solution.py:135
  237.4 5.0 reshape.401
  242.3 4.1 copy.88
  246.4 3.9 reshape.402
  259.9 64.6 %all-reduce = (f32[32,64]{1,0:T(8,128)S(1)}, f32[64]{0:T(128)S(1)}) all-reduce(f32[32,64]{1,0:T(8,128)S(1)} %fusion.53, f32[64]{0:T(128)S(1)} %get-tuple-element.41), channel_id=1, replica_groups=mesh['seq'=64,'chan'=2] {'seq','chan'}, use_global_device_ids=true, to_apply=%region_0.1 | all-reduce | flops 2112 | bytes 16896 | tf_op jit(solution)/shard_map/psum | solution.py:152
  325.1 5.9 all-to-all-start.3
  331.5 280.7 %psum.23 = f32[64,64]{1,0:T(8,128)S(1)} all-reduce(f32[64,64]{1,0:T(8,128)S(1)} %fusion.40), channel_id=1, replica_groups=mesh['seq'=64,'chan'=2] {'seq'}, use_global_device_ids=true, to_apply=%region_3.4 | all-reduce | flops 4096 | bytes 32768 | tf_op jit(solution)/shard_map/psum | solution.py:151
  (101 shorter events, 93.5 us)
Async XLA Ops:
  0.6 18.3 %copy-start = (f32[64,64]{1,0:T(8,128)S(1)}, f32[64,64]{1,0:T(8,128)}, u32[]{:S(2)}) copy-start(f32[64,64]{1,0:T(8,128)} %param.12) | copy-start | bytes 49156
  4.4 19.8 %all-to-all-start = ((bf16[64,2,1024]{2,1,0:T(2,128)(2,1)}), bf16[64,2,1024]{2,1,0:T(2,128)(2,1)S(1)}, u32[]{:S(2)}, u32[]{:S(2)}) async-start(bf16[64,2,1024]{2,1,0:T(2,128)(2,1)} %pad_maximum_fusion.14), calls=%async_computation | async-start | bytes 524288 | tf_op jit(solution)/shard_map/all_to_all | solution.py:60
  16.2 2.7 copy-start.13
  33.4 46.6 %all-to-all-start.1 = ((f32[128,2,3,1024]{3,1,2,0:T(2,128)}), f32[128,2,3,1024]{3,1,2,0:T(2,128)S(1)}, u32[]{:S(2)}, u32[]{:S(2)}) async-start(f32[128,2,3,1024]{3,1,2,0:T(2,128)} %copy.76), calls=%async_computation.1 | async-start | bytes 6291456 | tf_op jit(solution)/shard_map/all_to_all | solution.py:77
  41.2 0.6 copy-start.15
  109.9 5.5 copy-start.1
  110.0 5.5 copy-start.2
  110.0 5.5 copy-start.3
  126.2 6.8 %copy-start.6 = (f32[64,2,1,16,64]{4,3,2,1,0:T(8,128)}, f32[64,2,1,16,64]{4,3,2,1,0:T(8,128)S(1)}, u32[]{:S(2)}) copy-start(f32[64,2,1,16,64]{4,3,2,1,0:T(8,128)S(1)} %get-tuple-element.13) | copy-start | bytes 1572868
  126.9 6.0 copy-start.4
  126.9 6.0 copy-start.5
  148.9 4.6 copy-start.7
  148.9 4.6 copy-start.10
  148.9 4.6 copy-start.11
  171.9 7.0 %copy-start.8 = (f32[64,2,1024]{2,1,0:T(2,128)S(1)}, f32[64,2,1024]{2,1,0:T(2,128)}, u32[]{:S(2)}) copy-start(f32[64,2,1024]{2,1,0:T(2,128)} %get-tuple-element.25) | copy-start | bytes 1572868
  171.9 7.0 %copy-start.9 = (f32[64,2,1024]{2,1,0:T(2,128)S(1)}, f32[64,2,1024]{2,1,0:T(2,128)}, u32[]{:S(2)}) copy-start(f32[64,2,1024]{2,1,0:T(2,128)} %get-tuple-element.26) | copy-start | bytes 1572868
  187.5 46.3 %all-to-all-start.2 = ((f32[64,2,2,3,1024]{4,2,3,1,0:T(2,128)}), f32[64,2,2,3,1024]{4,2,3,1,0:T(2,128)S(1)}, u32[]{:S(2)}, u32[]{:S(2)}) async-start(f32[64,2,2,3,1024]{4,2,3,1,0:T(2,128)} %copy.86), calls=%async_computation.2 | async-start | bytes 6291456 | tf_op jit(solution)/shard_map/all_to_all | solution.py:135
  254.0 4.2 copy-start.12
  254.0 5.6 copy-start.14
  325.1 287.8 %all-to-all-start.3 = ((bf16[64,2,1024]{2,1,0:T(2,128)(2,1)}), bf16[64,2,1024]{2,1,0:T(2,128)(2,1)S(1)}, u32[]{:S(2)}, u32[]{:S(2)}) async-start(bf16[64,2,1024]{2,1,0:T(2,128)(2,1)} %slice.117), calls=%async_computation.3 | async-start | bytes 524288 | tf_op jit(solution)/shard_map/all_to_all | solution.py:140
where the time goes:
time: 627 us; the launch traced here: 616 us
  blocking collectives  345 us (55%)
  local copies, waits for them, and re-layouts  80.4 us (13%)
  waiting for transfers between devices  64.5 us (10%)
  matrix products  58.9 us (9%)
  other arithmetic  35.8 us (6%)
  starting transfers between devices  29.3 us (5%)
    psum x1, blocking collectives, local(): out_sum = lax.psum(out_part, 'seq')  281 us
    psum x1, blocking collectives, local(): embed_all, bias_all = lax.psum((embed_part, bias_part), ('seq', 'chan'))  64.6 us
    all_to_all x1, waiting for transfers between devices, local(): back = lax.all_to_all(back, 'seq', split_axis=0, concat_axis=0, tiled=True)  38.9 us
    dot_general x8, matrix products, blk_mix(): jnp.einsum('mb,qkzbc->qkzmc', table, vals, preferred_element_type=jnp.flo...  32.6 us
    dot_general x10, matrix products, mat_dot(): jnp.dot(lhs_mat, rhs_mat, preferred_element_type=jnp.float32, precision=e...  26.2 us
    all_to_all x1, waiting for transfers between devices, local(): spec = lax.all_to_all(spec, 'seq', split_axis=0, concat_axis=0, tiled=True)  23.2 us
  transfers between devices with their start and end apart: 4, of which 3 were waited for; matrix products, arithmetic and copies ran while one was open for 4% of the time, Pallas kernels for 0%

commit v1 on v0

--- a/solution.py
+++ b/solution.py
@@ -149,7 +149,7 @@
     embed_part = mat_dot(features.T, d_preact)
     bias_part = jnp.sum(d_preact, axis=0)
     out_sum = lax.psum(out_part, "seq")
-    embed_all, bias_all = lax.psum((embed_part, bias_part), ("seq", "chan"))
+    embed_all, bias_all = lax.psum(lax.psum((embed_part, bias_part), "chan"), "seq")
     norm_scale = 1.0 / math.sqrt(seq_total)
     return (conv_out, d_signal, embed_all * norm_scale, bias_all * norm_scale, out_sum * norm_scale)
 

time: 627 us -> 576 us (0.919)
  the two profiles are of different devices: /device:TPU:0 before, /device:TPU:1 now
where the time goes in v1:
time: 576 us; the launch traced here: 565 us
  blocking collectives  280 us (49%)
  local copies, waits for them, and re-layouts  80.5 us (14%)
  waiting for transfers between devices  73.5 us (13%)
  matrix products  58.9 us (10%)
  other arithmetic  35.8 us (6%)
  starting transfers between devices  34.9 us (6%)
    psum x1, blocking collectives, local(): lax.psum(lax.psum((embed_part, bias_part), 'chan'), 'seq')  270 us
    all_to_all x1, waiting for transfers between devices, local(): back = lax.all_to_all(back, 'seq', split_axis=0, concat_axis=0, tiled=True)  39.3 us
    dot_general x8, matrix products, blk_mix(): jnp.einsum('mb,qkzbc->qkzmc', table, vals, preferred_element_type=jnp.flo...  32.7 us
    dot_general x10, matrix products, mat_dot(): jnp.dot(lhs_mat, rhs_mat, preferred_element_type=jnp.float32, precision=e...  26.2 us
    all_to_all x1, waiting for transfers between devices, local(): spec = lax.all_to_all(spec, 'seq', split_axis=0, concat_axis=0, tiled=True)  23.7 us
  transfers between devices with their start and end apart: 4, of which 4 were waited for; matrix products, arithmetic and copies ran while one was open for 4% of the time, Pallas kernels for 0%

profile of v1, /device:TPU:1, one launch (start us, length us, event | category | flops | bytes accessed | tf_op | source)
XLA Modules:
  0.0 565.0 jit_solution(8643069451464559887)
XLA Ops:
  4.4 10.8 %all-to-all-start = ((bf16[64,2,1024]{2,1,0:T(2,128)(2,1)}), bf16[64,2,1024]{2,1,0:T(2,128)(2,1)S(1)}, u32[]{:S(2)}, u32[]{:S(2)}) async-start(bf16[64,2,1024]{2,1,0:T(2,128)(2,1)} %pad_maximum_fusion.14), calls=%async_computation | async-start | bytes 524288 | tf_op jit(solution)/shard_map/all_to_all | solution.py:60
  29.9 4.1 copy.76
  34.0 7.2 %all-to-all-start.1 = ((f32[128,2,3,1024]{3,1,2,0:T(2,128)}), f32[128,2,3,1024]{3,1,2,0:T(2,128)S(1)}, u32[]{:S(2)}, u32[]{:S(2)}) async-start(f32[128,2,3,1024]{3,1,2,0:T(2,128)} %copy.76), calls=%async_computation.1 | async-start | bytes 6291456 | tf_op jit(solution)/shard_map/all_to_all | solution.py:77
  48.2 9.5 %fusion.38 = (f32[64,2,1024]{2,1,0:T(2,128)}, f32[64,2,1024]{2,1,0:T(2,128)}) fusion(s32[2]{0:T(128)S(1)} %iota_add_fusion.1, s32[64,1024]{1,0:T(8,128)S(1)} %broadcast_add_fusion), kind=kLoop, calls=%fused_computation.88 | loop fusion | flops 1835008 | bytes 1310728 | tf_op jit(solution)/shard_map/cos | solution.py:130
  57.7 23.7 %all-to-all-done.1 = f32[128,2,3,1024]{3,1,2,0:T(2,128)S(1)} async-done(((f32[128,2,3,1024]{3,1,2,0:T(2,128)}), f32[128,2,3,1024]{3,1,2,0:T(2,128)S(1)}, u32[]{:S(2)}, u32[]{:S(2)}) %all-to-all-start.1) | async-done | bytes 3145760 | tf_op jit(solution)/shard_map/all_to_all | solution.py:77
  85.1 4.3 reshape.397
  93.2 9.4 %fusion = f32[2,64,2,2,3,1024]{5,1,4,3,2,0:T(8,128)S(1)} fusion(f32[2,64,64,1,1,1]{2,1,5,4,3,0:T(8,128)} %bitcast.98, f32[2,2,3,1024,64]{3,2,1,0,4:T(4,128)} %dot_general.72), kind=kOutput, calls=%fused_computation.6 | convolution fusion | flops 1207959552 | bytes 9469952 | tf_op jit(solution)/shard_map/dot_general | solution.py:11
  111.4 5.5 fusion.51
  134.4 4.7 subtract_bitcast_fusion
  139.0 4.9 reshape.411
  143.9 6.4 %add_bitcast_fusion = f32[64,2,3,16,64]{4,3,2,1,0:T(8,128)} fusion(f32[64,2,3,64,16]{3,4,2,1,0:T(8,128)S(1)} %fusion.3, f32[64,2,1,16,64]{4,3,2,1,0:T(8,128)} %copy-done.5, f32[64,2,1,16,64]{4,3,2,1,0:T(8,128)} %copy-done.6, f32[64,2,1,16,64]{4,3,2,1,0:T(8,128)} %copy-done.4), kind=kOutput, calls=%fused_computation.9 | convolution fusion | flops 76680704 | bytes 4718592 | tf_op jit(solution)/shard_map/mb,qkzbc->qkzmc/dot_general | solution.py:91
  150.3 4.6 reshape.412
  158.6 4.1 copy.85
  162.7 5.0 reshape.400
  176.4 3.9 squeeze.5
  184.3 4.7 copy.86
  188.9 6.3 %all-to-all-start.2 = ((f32[64,2,2,3,1024]{4,2,3,1,0:T(2,128)}), f32[64,2,2,3,1024]{4,2,3,1,0:T(2,128)S(1)}, u32[]{:S(2)}, u32[]{:S(2)}) async-start(f32[64,2,2,3,1024]{4,2,3,1,0:T(2,128)} %copy.86), calls=%async_computation.2 | async-start | bytes 6291456 | tf_op jit(solution)/shard_map/all_to_all | solution.py:135
  196.0 39.3 %all-to-all-done.2 = f32[64,2,2,3,1024]{4,2,3,1,0:T(2,128)S(1)} async-done(((f32[64,2,2,3,1024]{4,2,3,1,0:T(2,128)}), f32[64,2,2,3,1024]{4,2,3,1,0:T(2,128)S(1)}, u32[]{:S(2)}, u32[]{:S(2)}) %all-to-all-start.2) | async-done | bytes 3145760 | tf_op jit(solution)/shard_map/all_to_all | solution.py:135
  238.9 5.0 reshape.401
  243.8 4.1 copy.88
  261.4 9.4 %all-reduce.1 = (f32[32,64]{1,0:T(8,128)S(1)}, f32[64]{0:T(128)S(1)}) all-reduce(f32[32,64]{1,0:T(8,128)S(1)} %fusion.53, f32[64]{0:T(128)S(1)} %get-tuple-element.44), channel_id=1, replica_groups=mesh['seq'=64,'chan'=2] {'chan'}, use_global_device_ids=true, to_apply=%region_0.1 | all-reduce | flops 2112 | bytes 16896 | tf_op jit(solution)/shard_map/psum | solution.py:152
  270.8 270.4 %all-reduce = (f32[32,64]{1,0:T(8,128)S(1)}, f32[64]{0:T(128)S(1)}, f32[64,64]{1,0:T(8,128)S(1)}) all-reduce(f32[32,64]{1,0:T(8,128)S(1)} %get-tuple-element.10, f32[64]{0:T(128)S(1)} %get-tuple-element.11, f32[64,64]{1,0:T(8,128)S(1)} %fusion.40), channel_id=1, replica_groups=mesh['seq'=64,'chan'=2] {'seq'}, use_global_device_ids=true, to_apply=%region_1.2 | all-reduce | flops 6208 | bytes 49664 | tf_op jit(solution)/shard_map/psum | solution.py:152
  541.8 10.6 %all-to-all-start.3 = ((bf16[64,2,1024]{2,1,0:T(2,128)(2,1)}), bf16[64,2,1024]{2,1,0:T(2,128)(2,1)S(1)}, u32[]{:S(2)}, u32[]{:S(2)}) async-start(bf16[64,2,1024]{2,1,0:T(2,128)(2,1)} %slice.117), calls=%async_computation.3 | async-start | bytes 524288 | tf_op jit(solution)/shard_map/all_to_all | solution.py:140
  553.5 8.6 %all-to-all-done.3 = bf16[64,2,1024]{2,1,0:T(2,128)(2,1)S(1)} async-done(((bf16[64,2,1024]{2,1,0:T(2,128)(2,1)}), bf16[64,2,1024]{2,1,0:T(2,128)(2,1)S(1)}, u32[]{:S(2)}, u32[]{:S(2)}) %all-to-all-start.3) | async-done | bytes 262176 | tf_op jit(solution)/shard_map/all_to_all | solution.py:140
  (101 shorter events, 97.1 us)
Async XLA Ops:
  0.6 19.2 %copy-start = (f32[64,64]{1,0:T(8,128)S(1)}, f32[64,64]{1,0:T(8,128)}, u32[]{:S(2)}) copy-start(f32[64,64]{1,0:T(8,128)} %param.12) | copy-start | bytes 49156
  4.4 20.4 %all-to-all-start = ((bf16[64,2,1024]{2,1,0:T(2,128)(2,1)}), bf16[64,2,1024]{2,1,0:T(2,128)(2,1)S(1)}, u32[]{:S(2)}, u32[]{:S(2)}) async-start(bf16[64,2,1024]{2,1,0:T(2,128)(2,1)} %pad_maximum_fusion.14), calls=%async_computation | async-start | bytes 524288 | tf_op jit(solution)/shard_map/all_to_all | solution.py:60
  17.2 2.7 copy-start.13
  34.0 47.4 %all-to-all-start.1 = ((f32[128,2,3,1024]{3,1,2,0:T(2,128)}), f32[128,2,3,1024]{3,1,2,0:T(2,128)S(1)}, u32[]{:S(2)}, u32[]{:S(2)}) async-start(f32[128,2,3,1024]{3,1,2,0:T(2,128)} %copy.76), calls=%async_computation.1 | async-start | bytes 6291456 | tf_op jit(solution)/shard_map/all_to_all | solution.py:77
  42.2 0.6 copy-start.15
  111.4 5.5 copy-start.1
  111.4 5.5 copy-start.2
  111.4 5.5 copy-start.3
  127.6 6.8 %copy-start.6 = (f32[64,2,1,16,64]{4,3,2,1,0:T(8,128)}, f32[64,2,1,16,64]{4,3,2,1,0:T(8,128)S(1)}, u32[]{:S(2)}) copy-start(f32[64,2,1,16,64]{4,3,2,1,0:T(8,128)S(1)} %get-tuple-element.16) | copy-start | bytes 1572868
  128.3 6.0 %copy-start.4 = (f32[64,2,1,16,64]{4,3,2,1,0:T(8,128)}, f32[64,2,1,16,64]{4,3,2,1,0:T(8,128)S(1)}, u32[]{:S(2)}) copy-start(f32[64,2,1,16,64]{4,3,2,1,0:T(8,128)S(1)} %get-tuple-element.12) | copy-start | bytes 1572868
  128.3 6.0 %copy-start.5 = (f32[64,2,1,16,64]{4,3,2,1,0:T(8,128)}, f32[64,2,1,16,64]{4,3,2,1,0:T(8,128)S(1)}, u32[]{:S(2)}) copy-start(f32[64,2,1,16,64]{4,3,2,1,0:T(8,128)S(1)} %get-tuple-element.13) | copy-start | bytes 1572868
  150.3 4.6 copy-start.7
  150.3 4.6 copy-start.10
  150.3 4.6 copy-start.11
  173.3 7.0 %copy-start.8 = (f32[64,2,1024]{2,1,0:T(2,128)S(1)}, f32[64,2,1024]{2,1,0:T(2,128)}, u32[]{:S(2)}) copy-start(f32[64,2,1024]{2,1,0:T(2,128)} %get-tuple-element.28) | copy-start | bytes 1572868
  173.3 7.0 %copy-start.9 = (f32[64,2,1024]{2,1,0:T(2,128)S(1)}, f32[64,2,1024]{2,1,0:T(2,128)}, u32[]{:S(2)}) copy-start(f32[64,2,1024]{2,1,0:T(2,128)} %get-tuple-element.29) | copy-start | bytes 1572868
  188.9 46.3 %all-to-all-start.2 = ((f32[64,2,2,3,1024]{4,2,3,1,0:T(2,128)}), f32[64,2,2,3,1024]{4,2,3,1,0:T(2,128)S(1)}, u32[]{:S(2)}, u32[]{:S(2)}) async-start(f32[64,2,2,3,1024]{4,2,3,1,0:T(2,128)} %copy.86), calls=%async_computation.2 | async-start | bytes 6291456 | tf_op jit(solution)/shard_map/all_to_all | solution.py:135
  255.4 4.2 copy-start.12
  255.4 5.6 copy-start.14
  541.8 20.3 %all-to-all-start.3 = ((bf16[64,2,1024]{2,1,0:T(2,128)(2,1)}), bf16[64,2,1024]{2,1,0:T(2,128)(2,1)S(1)}, u32[]{:S(2)}, u32[]{:S(2)}) async-start(bf16[64,2,1024]{2,1,0:T(2,128)(2,1)} %slice.117), calls=%async_computation.3 | async-start | bytes 524288 | tf_op jit(solution)/shard_map/all_to_all | solution.py:140
